TPU v7x, 32 devices: a whole 2x2x4 slice. The times are simulated.
32 devices in a mesh: ctx: 4 (over y, x), tp: 8 (over z, core).
Axes of the slice: x: 2, y: 2, z: 4, core: 2. Of those that a mesh axis runs over, the one named last changes fastest.
Arguments:
- resid: bfloat16 [1024, 4096], P('ctx', 'tp'), may hold values from -6 to 6
- attn_gain: bfloat16 [4096], replicated, may hold values from 0.5 to 1.5
- mlp_gain: bfloat16 [4096], replicated, may hold values from 0.5 to 1.5
- w_query: bfloat16 [4096, 4096], P(None, 'tp'), may hold values from -0.09375 to 0.09375
- w_kv: bfloat16 [4096, 1024], P(None, 'tp'), may hold values from -0.09375 to 0.09375
- w_out: bfloat16 [4096, 4096], P('tp'), may hold values from -0.09375 to 0.09375
- w_gate: bfloat16 [4096, 11008], P(None, 'tp'), may hold values from -0.09375 to 0.09375
- w_up: bfloat16 [4096, 11008], P(None, 'tp'), may hold values from -0.09375 to 0.09375
- w_down: bfloat16 [11008, 4096], P('tp'), may hold values from -0.0546875 to 0.0546875
- kv_cache: bfloat16 [32, 128, 1024], P('ctx'), may hold values from -70 to 70
- cache_len: int32 [4], replicated, may hold values from 1 to 2048
- span_len: int32 [4], replicated, may hold values from 1 to 256
- slot_req: int32 [32], P('ctx'), may hold values from 0 to 4, as said below
- slot_blk: int32 [32], P('ctx'), may hold values from 0 to 15, as said below
Outputs:
- layer_out: bfloat16 [1024, 4096], P('ctx', 'tp')
- new_kv: bfloat16 [1024, 1024], P('ctx', 'tp')
Inputs may be any that keep to these rules, and one draw needn't show every extreme that they name: `slot_req`: each request r holds ceil(cache_len[r] / 128) blocks, and each of its blocks stands in exactly one slot; every other slot is empty. `slot_blk`: block numbers of live slots are below their request's block count; empty slots carry 0.
All inputs are finite; a program needn't handle non-finite values.
Results may differ from a plain program's by a relative error of at most 0.035.
Values may be sent and summed in bfloat16 or wider, within the bound.
No kernel may reach another device: no remote copies, remote signals or barrier semaphores. Data moves between devices by JAX's collectives and lax.ppermute only.
A program may use at most 128 MiB of HBM per device.

v0:
```python
import jax
import jax.numpy as jnp
from jax import lax
from jax.sharding import PartitionSpec as P

HQ = 32
KVH = 4
HD = 128
BLK = 128
THETA = 5000000.0
EPS = 1e-05
NEG = -1e30


def rms_norm(values, gain):
    wide = values.astype(jnp.float32)
    factor = lax.rsqrt(jnp.mean(wide * wide, axis=-1, keepdims=True) + EPS)
    return (wide * factor * gain.astype(jnp.float32)).astype(jnp.bfloat16)


def rotate(vectors, positions):
    width = vectors.shape[-1]
    half = width // 2
    freqs = THETA ** (-(jnp.arange(half, dtype=jnp.float32) * 2.0 / width))
    angles = positions.astype(jnp.float32)[:, None] * freqs[None, :]
    cosine = jnp.cos(angles)[:, None, :]
    sine = jnp.sin(angles)[:, None, :]
    first = vectors[..., :half]
    second = vectors[..., half:]
    return jnp.concatenate(
        [first * cosine - second * sine, second * cosine + first * sine], axis=-1
    )


def column_term(rows, weight):
    return lax.dot_general(
        weight, rows, (((0,), (1,)), ((), ())), preferred_element_type=jnp.float32
    )


def gather_ctx(value, count):
    parts = [value]
    for shift in range(1, count):
        pairs = [(i, (i + shift) % count) for i in range(count)]
        parts.append(lax.ppermute(value, "ctx", pairs))
    return parts


def per_device(
    resid,
    attn_gain,
    mlp_gain,
    w_query,
    w_kv,
    w_out,
    w_gate,
    w_up,
    w_down,
    kv_cache,
    cache_len,
    span_len,
    slot_req,
    slot_blk,
):
    span_size = resid.shape[0]
    ctx_count = lax.axis_size("ctx")
    q_cols = w_query.shape[1]
    heads_dev = q_cols // HD
    ctx_rank = lax.axis_index("ctx")
    tp_rank = lax.axis_index("tp")
    group = tp_rank * heads_dev // (HQ // KVH)
    my_len = cache_len[ctx_rank]
    my_span = span_len[ctx_rank]
    offsets = jnp.arange(span_size, dtype=jnp.int32)
    positions = my_len + offsets
    live_rows = offsets < my_span
    own_cache = jnp.concatenate(
        [
            lax.dynamic_slice_in_dim(kv_cache, group * HD, HD, 2),
            lax.dynamic_slice_in_dim(kv_cache, KVH * HD + group * HD, HD, 2),
        ],
        axis=2,
    )
    own_meta = jnp.stack([slot_req, slot_blk])
    cache_all = jnp.concatenate(gather_ctx(own_cache, ctx_count), axis=0)
    meta_all = jnp.concatenate(gather_ctx(own_meta, ctx_count), axis=1)
    full_resid = lax.all_gather(resid, "tp", axis=1, tiled=True)
    x_norm = rms_norm(full_resid, attn_gain)
    query = rotate(
        jnp.dot(x_norm, w_query, preferred_element_type=jnp.float32).reshape(
            span_size, heads_dev, HD
        ),
        positions,
    ).astype(jnp.bfloat16)
    kv_piece = jnp.dot(x_norm, w_kv, preferred_element_type=jnp.float32).astype(jnp.bfloat16)
    kv_width = kv_piece.shape[1]
    kv_all = lax.all_gather(kv_piece, "tp", axis=1, tiled=True)
    all_keys = rotate(
        kv_all[:, : KVH * HD].astype(jnp.float32).reshape(span_size, KVH, HD), positions
    ).astype(jnp.bfloat16)
    joined = jnp.concatenate([all_keys.reshape(span_size, KVH * HD), kv_all[:, KVH * HD :]], axis=1)
    mine = lax.dynamic_slice_in_dim(joined, tp_rank * kv_width, kv_width, 1)
    new_kv = jnp.where(live_rows[:, None], mine, jnp.zeros_like(mine))
    new_keys = lax.dynamic_index_in_dim(all_keys, group, 1, keepdims=False)
    new_vals = lax.dynamic_slice_in_dim(kv_all, KVH * HD + group * HD, HD, 1)
    cache_rows = cache_all.shape[0] * BLK
    keys = jnp.concatenate([cache_all[..., :HD].reshape(cache_rows, HD), new_keys], axis=0)
    vals = jnp.concatenate([cache_all[..., HD:].reshape(cache_rows, HD), new_vals], axis=0)
    key_pos = meta_all[1][:, None] * BLK + jnp.arange(BLK, dtype=jnp.int32)[None, :]
    cache_ok = ((meta_all[0][:, None] == ctx_rank) & (key_pos < my_len)).reshape(cache_rows)
    new_ok = (offsets[None, :] <= offsets[:, None]) & (offsets[None, :] < my_span)
    valid = jnp.concatenate(
        [jnp.broadcast_to(cache_ok[None, :], (span_size, cache_rows)), new_ok], axis=1
    )
    scores = jnp.einsum("chd,kd->hck", query, keys, preferred_element_type=jnp.float32) * HD ** (
        -0.5
    )
    peak = jnp.max(jnp.where(valid[None], scores, NEG), axis=2)
    weights = jnp.where(valid[None], jnp.exp(scores - peak[..., None]), 0.0)
    total = jnp.sum(weights, axis=2)
    summed = jnp.einsum(
        "hck,kd->hcd", weights.astype(jnp.bfloat16), vals, preferred_element_type=jnp.float32
    )
    attn_rows = (
        (summed / total[..., None])
        .transpose(1, 0, 2)
        .reshape(span_size, q_cols)
        .astype(jnp.bfloat16)
    )
    head_sum = lax.psum(
        jnp.dot(attn_rows, w_out, preferred_element_type=jnp.float32).astype(jnp.bfloat16), "tp"
    )
    full_mid = (full_resid.astype(jnp.float32) + head_sum.astype(jnp.float32)).astype(jnp.bfloat16)
    mid = lax.dynamic_slice_in_dim(full_mid, tp_rank * resid.shape[1], resid.shape[1], 1)
    x_two = rms_norm(full_mid, mlp_gain)
    gate = jnp.dot(x_two, w_gate, preferred_element_type=jnp.float32)
    up_part = jnp.dot(x_two, w_up, preferred_element_type=jnp.float32)
    hidden = (jax.nn.silu(gate) * up_part).astype(jnp.bfloat16)
    down_sum = lax.psum_scatter(
        column_term(hidden, w_down).astype(jnp.bfloat16), "tp", scatter_dimension=0, tiled=True
    ).astype(jnp.float32)
    layer_out = (mid.astype(jnp.float32) + down_sum.T).astype(jnp.bfloat16)
    layer_out = jnp.where(live_rows[:, None], layer_out, jnp.zeros_like(layer_out))
    return (layer_out, new_kv)


def solution(mesh):
    return jax.shard_map(
        per_device,
        mesh=mesh,
        in_specs=(
            P("ctx", "tp"),
            P(),
            P(),
            P(None, "tp"),
            P(None, "tp"),
            P("tp", None),
            P(None, "tp"),
            P(None, "tp"),
            P("tp", None),
            P("ctx", None, None),
            P(),
            P(),
            P("ctx"),
            P("ctx"),
        ),
        out_specs=(P("ctx", "tp"), P("ctx", "tp")),
        check_vma=False,
    )
```

profile of v0, /device:TPU:0, one launch (start us, length us, event | category | flops | bytes accessed | tf_op | source)
XLA Modules:
  0.0 248.4 jit_solution(2127436485068741131)
XLA Ops:
  8.6 3.9 %collective-permute-start.2 = (s32[2,8]{1,0:T(2,128)S(1)}, s32[2,8]{1,0:T(2,128)S(1)}, u32[]{:S(2)}, u32[]{:S(2)}) collective-permute-start(s32[2,8]{1,0:T(2,128)S(1)} %pad_add_fusion.1), channel_id=1, source_target_pairs={{0,24},{8,0},{16,8},{24,16},{1,25},{9,1},{17,9},{25,17},{2,26},{10... | collective-permute-start | bytes 200 | tf_op jit(solution)/shard_map/ppermute | solution.py:45
  13.6 1.1 constant_dynamic-slice_fusion.2
  14.8 2.4 collective-permute-start.5
  17.2 1.5 collective-permute-start.4
  18.7 1.2 dynamic_slice.25
  19.9 1.3 dynamic_slice.26
  23.3 1.2 multiply_cosine_fusion
  24.5 0.8 pad_add_fusion.2
  26.0 5.1 %pad_add_fusion = pred[256,4352]{0,1:T(8,128)(4,1)} fusion(pred[256,256]{0,1:T(8,128)(4,1)S(1)} %fusion.45, pred[4352]{0:T(1024)(128)(4,1)S(1)} %pad.8.clone), kind=kLoop, calls=%fused_computation.20 | loop fusion | flops 1114112 | bytes 1184000 | tf_op jit(solution)/shard_map/concatenate | solution.py:112
  31.1 9.8 %collective-permute-done.4 = bf16[8,128,256]{2,1,0:T(8,128)(2,1)S(1)} collective-permute-done((bf16[8,128,256]{2,1,0:T(8,128)(2,1)S(1)}, bf16[8,128,256]{2,1,0:T(8,128)(2,1)S(1)}, u32[]{:S(2)}, u32[]{:S(2)}) %collective-permute-start.4) | collective-permute-done | bytes 524320 | tf_op jit(solution)/shard_map/ppermute | solution.py:45
  41.2 1.6 fusion.56
  42.8 1.3 copy.25
  44.1 2.2 fusion.14
  46.3 2.4 convolution_convert_fusion.2
  48.7 14.3 %all_gather.7 = bf16[256,1024]{1,0:T(8,128)(2,1)S(1)} all-gather(bf16[256,128]{1,0:T(8,128)(2,1)S(1)} %convolution_convert_fusion.2), channel_id=1, replica_groups=mesh['ctx'=4,'tp'=8] {'tp'}, dimensions={1}, use_global_device_ids=true | all-gather | bytes 589824 | tf_op jit(solution)/shard_map/all_gather | solution.py:97
  63.0 0.9 fusion.57
  63.9 0.7 copy.21
  64.7 3.5 %fusion.37 = f32[256,512]{1,0:T(8,128)S(1)} fusion(bf16[4096,512]{1,0:T(8,128)(2,1)} %param.17, bf16[256,4096]{1,0:T(8,128)(2,1)S(1)} %copy-done.2, f32[4096]{0:T(1024)S(1)} %convert_element_type.74, f32[256]{0:T(256)S(1)} %add_rsqrt_fusion.1), kind=kOutput, calls=%fused_computation.43 | convolution fusion | flops 1077936128 | bytes 6833152 | tf_op jit(solution)/shard_map/dot_general | solution.py:90
  68.4 1.2 reshape.161
  70.3 1.0 multiply_subtract_fusion
  71.5 1.0 subtract_convert_fusion
  72.6 8.7 %fusion.30 = f32[4352,256,4]{1,0,2:T(8,128)} fusion(bf16[256,128]{1,0:T(8,128)(2,1)S(1)} %dynamic-slice_bitcast_fusion, bf16[4096,128]{1,0:T(8,128)(2,1)S(1)} %bitcast.63, bf16[256,4,64]{2,0,1:T(8,128)(2,1)S(1)} %get-tuple-element.9, bf16[256,4,64]{2,0,1:T(8,128)(2,1)S(1)} %get-tuple-element.8), kind=kOutput, calls=%fused_computation.39 | convolution fusion | flops 1143603200 | bytes 19202048 | tf_op jit(solution)/shard_map/chd,kd->hck/dot_general | solution.py:115
  81.2 18.7 %fusion.60 = (f32[4,256]{1,0:T(4,128)S(1)}, bf16[4,256,4352]{1,2,0:T(8,128)(2,1)}) fusion(f32[4352,256,4]{1,0,2:T(8,128)} %fusion.30, pred[256,4352]{0,1:T(8,128)(4,1)} %pad_add_fusion), kind=kOutput, calls=%fused_computation.91 | output fusion | flops 31199488 | bytes 27856896 | tf_op jit(solution)/shard_map/sub | solution.py:119
  100.0 5.3 %fusion.25 = bf16[256,4,128]{0,2,1:T(8,128)(2,1)S(1)} fusion(bf16[4,256,4352]{1,2,0:T(8,128)(2,1)} %get-tuple-element.21, bf16[256,128]{0,1:T(8,128)(2,1)S(1)} %copy-done.8, bf16[4096,128]{0,1:T(8,128)(2,1)} %copy.25, f32[256,4]{0,1:T(4,128)S(1)} %bitcast.70), kind=kOutput, calls=%fused_computation.33 | convolution fusion | flops 1143341056 | bytes 10293248 | tf_op jit(solution)/shard_map/hck,kd->hcd/dot_general | solution.py:121
  105.3 2.7 %convolution_convert_fusion = bf16[256,4096]{1,0:T(8,128)(2,1)} fusion(bf16[256,512]{0,1:T(8,128)(2,1)S(1)} %bitcast.65, bf16[512,4096]{1,0:T(8,128)(2,1)S(1)} %copy-done.3), kind=kOutput, calls=%fused_computation.17 | convolution fusion | flops 1074790400 | bytes 6553600 | tf_op jit(solution)/shard_map/dot_general | solution.py:131
  108.1 63.7 %all-reduce.2.cloned.1.call-done = bf16[256,4096]{1,0:T(8,128)(2,1)} async-done(((bf16[256,4096]{1,0:T(8,128)(2,1)}), bf16[256,4096]{1,0:T(8,128)(2,1)}) %all-reduce.2.cloned.1.call-update) | async-done | bytes 2097168 | tf_op jit(solution)/shard_map/psum | solution.py:130
  171.8 3.9 %fusion.11 = (f32[256]{0:T(256)S(1)}, bf16[256,4096]{1,0:T(8,128)(2,1)}) fusion(bf16[256,4096]{1,0:T(8,128)(2,1)} %all-reduce.2.cloned.1.call-done, bf16[256,4096]{1,0:T(8,128)(2,1)S(1)} %copy-done.2), kind=kLoop, calls=%fused_computation.21 | loop fusion | flops 7339776 | bytes 6292480 | tf_op jit(solution)/shard_map/reduce_sum | solution.py:17
  175.7 7.0 %fusion.35 = f32[256,1376]{0,1:T(8,128)S(1)} fusion(bf16[4096,1376]{0,1:T(8,128)(2,1)} %param.20, bf16[256,4096]{1,0:T(8,128)(2,1)} %get-tuple-element.3, f32[4096]{0:T(1024)S(1)} %convert_element_type.87, f32[256]{0:T(256)S(1)} %add_rsqrt_fusion), kind=kOutput, calls=%fused_computation.42 | convolution fusion | flops 2889875456 | bytes 14795776 | tf_op jit(solution)/shard_map/dot_general | solution.py:136
  182.7 21.7 %fusion.10 = bf16[4096,256]{0,1:T(8,128)(2,1)} fusion(bf16[1376,4096]{1,0:T(8,128)(2,1)} %param.22, bf16[4096,1376]{0,1:T(8,128)(2,1)} %param.21, f32[256,1376]{0,1:T(8,128)S(1)} %fusion.35, bf16[256,4096]{1,0:T(8,128)(2,1)} %get-tuple-element.3, f32[4096]{0:T(1024)S(1)} %convert_element_type.87, f32[256]{0:T(256)S(1)} %add_rsqrt_fusion), kind=kOutput, calls=%fused_computation.19 | convolution fusion | flops 5778718720 | bytes 28165120 | tf_op jit(solution)/shard_map/dot_general | solution.py:36
  204.6 0.7 fusion.47
  205.4 34.7 %reduce-scatter.2.cloned.1.call-done = bf16[512,256]{0,1:T(8,128)(2,1)} async-done(((bf16[4096,256]{0,1:T(8,128)(2,1)}), bf16[512,256]{0,1:T(8,128)(2,1)}) %reduce-scatter.2.cloned.1.call-update) | async-done | bytes 262160 | tf_op jit(solution)/shard_map/reduce_scatter | solution.py:139
  240.1 1.8 fusion.41
  (57 shorter events, 7.1 us)
Async XLA Ops:
  7.2 39.1 %copy-start = (bf16[4096,128]{1,0:T(8,128)(2,1)S(1)}, bf16[4096,128]{1,0:T(8,128)(2,1)}, u32[]{:S(2)}) copy-start(bf16[4096,128]{1,0:T(8,128)(2,1)} %param.18) | copy-start | bytes 3145732
  7.2 36.9 %all-gather.2.cloned.1.call-start = ((), (), s32[]{:S(2)}) async-start(), calls=%async_computation.1 | async-start | bytes 2359296 | tf_op jit(solution)/shard_map/all_gather | solution.py:87
  7.9 163.9 %all-reduce.2.cloned.1.call-start = ((), (), s32[]{:S(2)}) async-start(), calls=%async_computation.2 | async-start | bytes 4194304 | tf_op jit(solution)/shard_map/psum | solution.py:130
  8.6 15.9 %collective-permute-start.2 = (s32[2,8]{1,0:T(2,128)S(1)}, s32[2,8]{1,0:T(2,128)S(1)}, u32[]{:S(2)}, u32[]{:S(2)}) collective-permute-start(s32[2,8]{1,0:T(2,128)S(1)} %pad_add_fusion.1), channel_id=1, source_target_pairs={{0,24},{8,0},{16,8},{24,16},{1,25},{9,1},{17,9},{25,17},{2,26},{10... | collective-permute-start | bytes 200 | tf_op jit(solution)/shard_map/ppermute | solution.py:45
  12.5 12.0 %collective-permute-start.1 = (s32[2,8]{1,0:T(2,128)S(1)}, s32[2,8]{1,0:T(2,128)S(1)}, u32[]{:S(2)}, u32[]{:S(2)}) collective-permute-start(s32[2,8]{1,0:T(2,128)S(1)} %pad_add_fusion.1), channel_id=1, source_target_pairs={{0,16},{8,24},{16,0},{24,8},{1,17},{9,25},{17,1},{25,9},{2,18},{10... | collective-permute-start | bytes 200 | tf_op jit(solution)/shard_map/ppermute | solution.py:45
  13.0 11.5 %collective-permute-start = (s32[2,8]{1,0:T(2,128)S(1)}, s32[2,8]{1,0:T(2,128)S(1)}, u32[]{:S(2)}, u32[]{:S(2)}) collective-permute-start(s32[2,8]{1,0:T(2,128)S(1)} %pad_add_fusion.1), channel_id=1, source_target_pairs={{0,8},{8,16},{16,24},{24,0},{1,9},{9,17},{17,25},{25,1},{2,10},{10... | collective-permute-start | bytes 200 | tf_op jit(solution)/shard_map/ppermute | solution.py:45
  14.8 16.4 %collective-permute-start.5 = (bf16[8,128,256]{2,1,0:T(8,128)(2,1)S(1)}, bf16[8,128,256]{2,1,0:T(8,128)(2,1)S(1)}, u32[]{:S(2)}, u32[]{:S(2)}) collective-permute-start(bf16[8,128,256]{2,1,0:T(8,128)(2,1)S(1)} %pad_maximum_fusion.1), channel_id=1, source_target_pairs={{0,24},{8,0},{16,8},{24,16},{1,25},{9,1},{17,9},{25,17},{2,26},{10... | collective-permute-start | bytes 1572872 | tf_op jit(solution)/shard_map/ppermute | solution.py:45
  17.2 23.8 %collective-permute-start.4 = (bf16[8,128,256]{2,1,0:T(8,128)(2,1)S(1)}, bf16[8,128,256]{2,1,0:T(8,128)(2,1)S(1)}, u32[]{:S(2)}, u32[]{:S(2)}) collective-permute-start(bf16[8,128,256]{2,1,0:T(8,128)(2,1)S(1)} %pad_maximum_fusion.1), channel_id=1, source_target_pairs={{0,16},{8,24},{16,0},{24,8},{1,17},{9,25},{17,1},{25,9},{2,18},{10... | collective-permute-start | bytes 1572872 | tf_op jit(solution)/shard_map/ppermute | solution.py:45
  24.5 16.4 %collective-permute-start.3 = (bf16[8,128,256]{2,1,0:T(8,128)(2,1)S(1)}, bf16[8,128,256]{2,1,0:T(8,128)(2,1)S(1)}, u32[]{:S(2)}, u32[]{:S(2)}) collective-permute-start(bf16[8,128,256]{2,1,0:T(8,128)(2,1)S(1)} %pad_maximum_fusion.1), channel_id=1, source_target_pairs={{0,8},{8,16},{16,24},{24,0},{1,9},{9,17},{17,25},{25,1},{2,10},{10... | collective-permute-start | bytes 1572872 | tf_op jit(solution)/shard_map/ppermute | solution.py:45
  44.1 20.6 %copy-start.2 = (bf16[256,4096]{1,0:T(8,128)(2,1)S(1)}, bf16[256,4096]{1,0:T(8,128)(2,1)}, u32[]{:S(2)}) copy-start(bf16[256,4096]{1,0:T(8,128)(2,1)} %all-gather.2.cloned.1.call-done) | copy-start | bytes 6291460
  69.6 3.0 %copy-start.4 = (bf16[32,128,128]{2,1,0:T(8,128)(2,1)S(1)}, bf16[32,128,128]{2,1,0:T(8,128)(2,1)}, u32[]{:S(2)}) copy-start(bf16[32,128,128]{2,1,0:T(8,128)(2,1)} %get-tuple-element.5) | copy-start | bytes 3145732
  71.3 9.9 %copy-start.5 = (bf16[256,4,64]{2,0,1:T(8,128)(2,1)}, bf16[256,4,64]{2,0,1:T(8,128)(2,1)S(1)}, u32[]{:S(2)}) copy-start(bf16[256,4,64]{2,0,1:T(8,128)(2,1)S(1)} %get-tuple-element.11) | copy-start | bytes 393220
  81.2 18.7 %copy-start.8 = (bf16[256,128]{0,1:T(8,128)(2,1)S(1)}, bf16[256,128]{0,1:T(8,128)(2,1)}, u32[]{:S(2)}) copy-start(bf16[256,128]{0,1:T(8,128)(2,1)} %copy.21) | copy-start | bytes 196612
  100.0 5.3 %copy-start.3 = (bf16[512,4096]{1,0:T(8,128)(2,1)S(1)}, bf16[512,4096]{1,0:T(8,128)(2,1)}, u32[]{:S(2)}) copy-start(bf16[512,4096]{1,0:T(8,128)(2,1)} %param.19) | copy-start | bytes 12582916
  105.3 2.7 %copy-start.9 = (bf16[4096]{0:T(1024)(128)(2,1)S(1)}, bf16[4096]{0:T(1024)(128)(2,1)}, u32[]{:S(2)}) copy-start(bf16[4096]{0:T(1024)(128)(2,1)} %param.16) | copy-start | bytes 24580
  108.0 132.1 %reduce-scatter.2.cloned.1.call-start = ((), (), s32[]{:S(2)}) async-start(), calls=%async_computation.3 | async-start | bytes 2359296 | tf_op jit(solution)/shard_map/reduce_scatter | solution.py:139
  182.7 21.8 %copy-start.6 = (bf16[256,4,64]{2,0,1:T(8,128)(2,1)S(1)}, bf16[256,4,64]{2,0,1:T(8,128)(2,1)}, u32[]{:S(2)}) copy-start(bf16[256,4,64]{2,0,1:T(8,128)(2,1)} %copy-done.5) | copy-start | bytes 393220
  182.7 21.9 %copy-start.7 = (bf16[256,512]{1,0:T(8,128)(2,1)S(1)}, bf16[256,512]{1,0:T(8,128)(2,1)}, u32[]{:S(2)}) copy-start(bf16[256,512]{1,0:T(8,128)(2,1)} %get-tuple-element.12) | copy-start | bytes 786436
  182.7 59.2 %copy-start.1 = (bf16[4096,128]{1,0:T(8,128)(2,1)S(1)}, bf16[4096,128]{1,0:T(8,128)(2,1)}, u32[]{:S(2)}) copy-start(bf16[4096,128]{1,0:T(8,128)(2,1)} %param.18) | copy-start | bytes 3145732
Sparse Core Ops, SparseCore 0:
  9.6 31.7 all-gather.1
  108.1 63.6 all-reduce.1
  204.6 35.4 reduce-scatter.1
where the time goes:
time: 249 us; the launch traced here: 248 us
  waiting for transfers between devices  109 us (44%)
  matrix products  51.2 us (21%)
  other arithmetic  41.7 us (17%)
  blocking collectives  14.3 us (6%)
  between operations  14 us (6%)
  local copies, waits for them, and re-layouts  9.32 us (4%)
  starting transfers between devices  9.02 us (4%)
    psum x1, waiting for transfers between devices, per_device(): lax.psum(jnp.dot(attn_rows, w_out, preferred_element_type=jnp.float32).as...  63.7 us
    reduce_scatter x1, waiting for transfers between devices, per_device(): lax.psum_scatter(column_term(hidden, w_down).astype(jnp.bfloat16), 'tp',...  34.7 us
    dot_general x1, matrix products, column_term(): lax.dot_general(weight, rows, (((0,), (1,)), ((), ())), preferred_element...  21.7 us
    sub x1, other arithmetic, per_device(): weights = jnp.where(valid[None], jnp.exp(scores - peak[..., None]), 0.0)  18.7 us
    all_gather x1, blocking collectives, per_device(): kv_all = lax.all_gather(kv_piece, 'tp', axis=1, tiled=True)  14.3 us
    ppermute x6, waiting for transfers between devices, gather_ctx(): parts.append(lax.ppermute(value, 'ctx', pairs))  9.82 us
    ppermute x6, starting transfers between devices, gather_ctx(): parts.append(lax.ppermute(value, 'ctx', pairs))  8.9 us
    dot_general x1, matrix products, per_device(): jnp.einsum('chd,kd->hck', query, keys, preferred_element_type=jnp.float32)  8.67 us
  transfers between devices with their start and end apart: 9, of which 3 were waited for; matrix products, arithmetic and copies ran while one was open for 7% of the time, Pallas kernels for 0%

commit v1 on v0

--- a/solution.py
+++ b/solution.py
@@ -94,7 +94,16 @@
     ).astype(jnp.bfloat16)
     kv_piece = jnp.dot(x_norm, w_kv, preferred_element_type=jnp.float32).astype(jnp.bfloat16)
     kv_width = kv_piece.shape[1]
-    kv_all = lax.all_gather(kv_piece, "tp", axis=1, tiled=True)
+    ways = lax.axis_size("tp")
+    up = [(d, (d + 1) % ways) for d in range(ways)]
+    down = [(d, (d - 1) % ways) for d in range(ways)]
+    earlier, later = ([kv_piece], [kv_piece])
+    for _ in range(ways // 2):
+        earlier.append(lax.ppermute(earlier[-1], "tp", up))
+    for _ in range((ways - 1) // 2):
+        later.append(lax.ppermute(later[-1], "tp", down))
+    line = jnp.concatenate([*earlier[::-1], *later[1:]], axis=1)
+    kv_all = jnp.roll(line, (lax.axis_index("tp") - ways // 2) * kv_piece.shape[1], axis=1)
     all_keys = rotate(
         kv_all[:, : KVH * HD].astype(jnp.float32).reshape(span_size, KVH, HD), positions
     ).astype(jnp.bfloat16)

time: 249 us -> 259 us (1.040)
  blocking collectives: 14.3 us -> 0 us
  starting transfers between devices: 9.02 us -> 19.8 us
  local copies, waits for them, and re-layouts: 9.32 us -> 18.9 us
  waiting for transfers between devices: 109 us -> 115 us
    all_gather x1 -> x0, blocking collectives: 14.3 us -> none  [per_device(): kv_all = lax.all_gather(kv_piece, 'tp', axis=1, tiled=True)]
    ppermute x0 -> x7, starting transfers between devices: none -> 10.7 us  [the longest x3 10.7 us: per_device(): later.append(lax.ppermute(later[-1], 'tp', down))]
    unnamed x20 -> x44, local copies, waits for them, and re-layouts: 0.05 us -> 10.1 us
    ppermute x0 -> x7, waiting for transfers between devices: none -> 4.97 us  [the longest x4 4.97 us: per_device(): earlier.append(lax.ppermute(earlier[-1], 'tp', up))]
  transfers between devices with their start and end apart: 9 -> 16, of which waited for: 3 -> 6; matrix products, arithmetic and copies ran while one was open for 7% -> 10% of each run, Pallas kernels for 0% -> 0%
where the time goes in v1:
time: 259 us
  waiting for transfers between devices  115 us (44%)
  matrix products  51.5 us (20%)
  other arithmetic  39.3 us (15%)
  starting transfers between devices  19.8 us (8%)
  local copies, waits for them, and re-layouts  18.9 us (7%)
  between operations  14.2 us (5%)
    psum x1, waiting for transfers between devices, per_device(): lax.psum(jnp.dot(attn_rows, w_out, preferred_element_type=jnp.float32).as...  64.4 us
    reduce_scatter x1, waiting for transfers between devices, per_device(): lax.psum_scatter(column_term(hidden, w_down).astype(jnp.bfloat16), 'tp',...  34.5 us
    dot_general x1, matrix products, column_term(): lax.dot_general(weight, rows, (((0,), (1,)), ((), ())), preferred_element...  21.7 us
    sub x1, other arithmetic, per_device(): weights = jnp.where(valid[None], jnp.exp(scores - peak[..., None]), 0.0)  18.7 us
    ppermute x3, starting transfers between devices, per_device(): later.append(lax.ppermute(later[-1], 'tp', down))  10.7 us
    ppermute x6, waiting for transfers between devices, gather_ctx(): parts.append(lax.ppermute(value, 'ctx', pairs))  10.4 us
    unnamed x44, local copies, waits for them, and re-layouts  10.1 us
    dot_general x1, matrix products, per_device(): jnp.einsum('chd,kd->hck', query, keys, preferred_element_type=jnp.float32)  9.74 us
  transfers between devices with their start and end apart: 16, of which 6 were waited for; matrix products, arithmetic and copies ran while one was open for 10% of the time, Pallas kernels for 0%

profile of v1, /device:TPU:0, one launch (start us, length us, event | category | flops | bytes accessed | tf_op | source)
XLA Modules:
  0.0 258.6 jit_solution(15608545377129027867)
XLA Ops:
  8.6 3.9 %collective-permute-start.2 = (s32[2,8]{1,0:T(2,128)S(1)}, s32[2,8]{1,0:T(2,128)S(1)}, u32[]{:S(2)}, u32[]{:S(2)}) collective-permute-start(s32[2,8]{1,0:T(2,128)S(1)} %pad_add_fusion.1), channel_id=1, source_target_pairs={{0,24},{8,0},{16,8},{24,16},{1,25},{9,1},{17,9},{25,17},{2,26},{10... | collective-permute-start | bytes 200 | tf_op jit(solution)/shard_map/ppermute | solution.py:45
  14.8 2.4 collective-permute-start.5
  17.2 1.5 collective-permute-start.4
  18.7 1.2 dynamic_slice.32
  19.9 1.3 dynamic_slice.33
  25.5 5.1 %pad_add_fusion = pred[256,4352]{0,1:T(8,128)(4,1)} fusion(pred[256,256]{0,1:T(8,128)(4,1)S(1)} %fusion.45, pred[4352]{0:T(1024)(128)(4,1)S(1)} %pad.8.clone), kind=kLoop, calls=%fused_computation.20 | loop fusion | flops 1114112 | bytes 1184000 | tf_op jit(solution)/shard_map/concatenate | solution.py:121
  30.6 10.4 %collective-permute-done.4 = bf16[8,128,256]{2,1,0:T(8,128)(2,1)S(1)} collective-permute-done((bf16[8,128,256]{2,1,0:T(8,128)(2,1)S(1)}, bf16[8,128,256]{2,1,0:T(8,128)(2,1)S(1)}, u32[]{:S(2)}, u32[]{:S(2)}) %collective-permute-start.4) | collective-permute-done | bytes 524320 | tf_op jit(solution)/shard_map/ppermute | solution.py:45
  41.0 1.4 pad_maximum_fusion
  42.4 2.2 fusion.14
  45.2 2.5 convolution_convert_fusion.2
  47.8 1.6 fusion.56
  49.4 1.3 copy.25
  50.7 3.5 %collective-permute-start.10 = (bf16[256,128]{0,1:T(8,128)(2,1)S(1)}, bf16[256,128]{0,1:T(8,128)(2,1)}, u32[]{:S(2)}, u32[]{:S(2)}) collective-permute-start(bf16[256,128]{0,1:T(8,128)(2,1)S(1)} %convolution_convert_fusion.2), channel_id=1, source_target_pairs={{0,7},{1,0},{2,1},{3,2},{4,3},{5,4},{6,5},{7,6},{8,15},{9,8},{10,9... | collective-permute-start | bytes 196616 | tf_op jit(solution)/shard_map/ppermute | solution.py:104
  54.2 3.5 %fusion.37 = f32[256,512]{1,0:T(8,128)S(1)} fusion(bf16[4096,512]{1,0:T(8,128)(2,1)} %param.17, bf16[256,4096]{1,0:T(8,128)(2,1)S(1)} %copy-done.2, f32[4096]{0:T(1024)S(1)} %convert_element_type.74, f32[256]{0:T(256)} %copy-done.12), kind=kOutput, calls=%fused_computation.43 | convolution fusion | flops 1077936128 | bytes 6833152 | tf_op jit(solution)/shard_map/dot_general | solution.py:90
  57.9 1.9 collective-permute-done.7
  60.2 3.6 %collective-permute-start.11 = (bf16[256,128]{0,1:T(8,128)(2,1)}, bf16[256,128]{0,1:T(8,128)(2,1)S(1)}, u32[]{:S(2)}, u32[]{:S(2)}) collective-permute-start(bf16[256,128]{0,1:T(8,128)(2,1)} %collective-permute-done.10), channel_id=1, source_target_pairs={{0,7},{1,0},{2,1},{3,2},{4,3},{5,4},{6,5},{7,6},{8,15},{9,8},{10,9... | collective-permute-start | bytes 196616 | tf_op jit(solution)/shard_map/ppermute | solution.py:104
  63.8 2.1 collective-permute-done.8
  66.8 3.5 %collective-permute-start.12 = (bf16[256,128]{0,1:T(8,128)(2,1)S(1)}, bf16[256,128]{0,1:T(8,128)(2,1)S(1)}, u32[]{:S(2)}, u32[]{:S(2)}) collective-permute-start(bf16[256,128]{0,1:T(8,128)(2,1)S(1)} %collective-permute-done.11), channel_id=1, source_target_pairs={{0,7},{1,0},{2,1},{3,2},{4,3},{5,4},{6,5},{7,6},{8,15},{9,8},{10,9... | collective-permute-start | bytes 196616 | tf_op jit(solution)/shard_map/ppermute | solution.py:104
  76.6 2.0 copy.27
  78.6 2.0 copy.26
  80.5 1.3 multiply_subtract_fusion
  82.1 9.7 %fusion.30 = f32[4352,256,4]{1,0,2:T(8,128)} fusion(bf16[256,128]{1,0:T(8,128)(2,1)S(1)} %dynamic-slice_bitcast_fusion, bf16[4096,128]{1,0:T(8,128)(2,1)S(1)} %bitcast.61, bf16[256,4,64]{2,0,1:T(8,128)(2,1)} %get-tuple-element.11, bf16[256,4,64]{2,0,1:T(8,128)(2,1)} %get-tuple-element.10), kind=kOutput, calls=%fused_computation.39 | convolution fusion | flops 1143603200 | bytes 19202048 | tf_op jit(solution)/shard_map/chd,kd->hck/dot_general | solution.py:124
  91.8 18.7 %fusion.59 = (f32[4,256]{1,0:T(4,128)S(1)}, bf16[4,256,4352]{1,2,0:T(8,128)(2,1)}) fusion(f32[4352,256,4]{1,0,2:T(8,128)} %fusion.30, pred[256,4352]{0,1:T(8,128)(4,1)} %pad_add_fusion), kind=kOutput, calls=%fused_computation.106 | output fusion | flops 31199488 | bytes 27856896 | tf_op jit(solution)/shard_map/sub | solution.py:128
  110.5 5.0 %fusion.25 = bf16[256,4,128]{0,2,1:T(8,128)(2,1)S(1)} fusion(bf16[4,256,4352]{1,2,0:T(8,128)(2,1)} %get-tuple-element.23, bf16[256,128]{0,1:T(8,128)(2,1)S(1)} %constant_dynamic-slice_fusion.1, bf16[4096,128]{0,1:T(8,128)(2,1)S(1)} %copy-done.8, f32[256,4]{0,1:T(4,128)S(1)} %bitcast.70), kind=kOutput, calls=%fused_computation.33 | convolution fusion | flops 1143341056 | bytes 10293248 | tf_op jit(solution)/shard_map/hck,kd->hcd/dot_general | solution.py:130
  115.6 2.6 %convolution_convert_fusion = bf16[256,4096]{1,0:T(8,128)(2,1)} fusion(bf16[256,512]{0,1:T(8,128)(2,1)S(1)} %bitcast.65, bf16[512,4096]{1,0:T(8,128)(2,1)S(1)} %copy-done.4), kind=kOutput, calls=%fused_computation.17 | convolution fusion | flops 1074790400 | bytes 6553600 | tf_op jit(solution)/shard_map/dot_general | solution.py:140
  118.3 64.4 %all-reduce.2.cloned.1.call-done = bf16[256,4096]{1,0:T(8,128)(2,1)} async-done(((bf16[256,4096]{1,0:T(8,128)(2,1)}), bf16[256,4096]{1,0:T(8,128)(2,1)}) %all-reduce.2.cloned.1.call-update) | async-done | bytes 2097168 | tf_op jit(solution)/shard_map/psum | solution.py:139
  182.6 2.5 fusion.11
  185.2 1.3 copy-done.6
  186.5 6.4 %fusion.35 = f32[256,1376]{0,1:T(8,128)S(1)} fusion(bf16[4096,1376]{0,1:T(8,128)(2,1)} %param.20, bf16[256,4096]{1,0:T(8,128)(2,1)S(1)} %get-tuple-element.5, f32[4096]{0:T(1024)S(1)} %convert_element_type.87, f32[256]{0:T(256)S(1)} %add_rsqrt_fusion), kind=kOutput, calls=%fused_computation.42 | convolution fusion | flops 2889875456 | bytes 14795776 | tf_op jit(solution)/shard_map/dot_general | solution.py:145
  192.9 21.7 %fusion.10 = bf16[4096,256]{0,1:T(8,128)(2,1)} fusion(bf16[1376,4096]{1,0:T(8,128)(2,1)} %param.22, bf16[4096,1376]{0,1:T(8,128)(2,1)} %param.21, f32[256,1376]{0,1:T(8,128)S(1)} %fusion.35, bf16[256,4096]{1,0:T(8,128)(2,1)} %copy-done.6, f32[4096]{0:T(1024)S(1)} %convert_element_type.87, f32[256]{0:T(256)S(1)} %add_rsqrt_fusion), kind=kOutput, calls=%fused_computation.19 | convolution fusion | flops 5778718720 | bytes 28165120 | tf_op jit(solution)/shard_map/dot_general | solution.py:36
  215.7 34.5 %reduce-scatter.2.cloned.1.call-done = bf16[512,256]{0,1:T(8,128)(2,1)} async-done(((bf16[4096,256]{0,1:T(8,128)(2,1)}), bf16[512,256]{0,1:T(8,128)(2,1)}) %reduce-scatter.2.cloned.1.call-update) | async-done | bytes 262160 | tf_op jit(solution)/shard_map/reduce_scatter | solution.py:148
  250.3 1.8 fusion.41
  (93 shorter events, 17.5 us)
Async XLA Ops:
  7.2 38.0 %copy-start = (bf16[4096,128]{1,0:T(8,128)(2,1)S(1)}, bf16[4096,128]{1,0:T(8,128)(2,1)}, u32[]{:S(2)}) copy-start(bf16[4096,128]{1,0:T(8,128)(2,1)} %param.18) | copy-start | bytes 3145732
  7.2 35.2 %all-gather.2.cloned.1.call-start = ((), (), s32[]{:S(2)}) async-start(), calls=%async_computation.1 | async-start | bytes 2359296 | tf_op jit(solution)/shard_map/all_gather | solution.py:87
  7.9 174.7 %all-reduce.2.cloned.1.call-start = ((), (), s32[]{:S(2)}) async-start(), calls=%async_computation.2 | async-start | bytes 4194304 | tf_op jit(solution)/shard_map/psum | solution.py:139
  8.6 15.2 %collective-permute-start.2 = (s32[2,8]{1,0:T(2,128)S(1)}, s32[2,8]{1,0:T(2,128)S(1)}, u32[]{:S(2)}, u32[]{:S(2)}) collective-permute-start(s32[2,8]{1,0:T(2,128)S(1)} %pad_add_fusion.1), channel_id=1, source_target_pairs={{0,24},{8,0},{16,8},{24,16},{1,25},{9,1},{17,9},{25,17},{2,26},{10... | collective-permute-start | bytes 200 | tf_op jit(solution)/shard_map/ppermute | solution.py:45
  12.5 11.4 %collective-permute-start.1 = (s32[2,8]{1,0:T(2,128)S(1)}, s32[2,8]{1,0:T(2,128)S(1)}, u32[]{:S(2)}, u32[]{:S(2)}) collective-permute-start(s32[2,8]{1,0:T(2,128)S(1)} %pad_add_fusion.1), channel_id=1, source_target_pairs={{0,16},{8,24},{16,0},{24,8},{1,17},{9,25},{17,1},{25,9},{2,18},{10... | collective-permute-start | bytes 200 | tf_op jit(solution)/shard_map/ppermute | solution.py:45
  13.0 10.9 %collective-permute-start = (s32[2,8]{1,0:T(2,128)S(1)}, s32[2,8]{1,0:T(2,128)S(1)}, u32[]{:S(2)}, u32[]{:S(2)}) collective-permute-start(s32[2,8]{1,0:T(2,128)S(1)} %pad_add_fusion.1), channel_id=1, source_target_pairs={{0,8},{8,16},{16,24},{24,0},{1,9},{9,17},{17,25},{25,1},{2,10},{10... | collective-permute-start | bytes 200 | tf_op jit(solution)/shard_map/ppermute | solution.py:45
  14.8 15.8 %collective-permute-start.5 = (bf16[8,128,256]{2,1,0:T(8,128)(2,1)S(1)}, bf16[8,128,256]{2,1,0:T(8,128)(2,1)S(1)}, u32[]{:S(2)}, u32[]{:S(2)}) collective-permute-start(bf16[8,128,256]{2,1,0:T(8,128)(2,1)S(1)} %pad_maximum_fusion.1), channel_id=1, source_target_pairs={{0,24},{8,0},{16,8},{24,16},{1,25},{9,1},{17,9},{25,17},{2,26},{10... | collective-permute-start | bytes 1572872 | tf_op jit(solution)/shard_map/ppermute | solution.py:45
  17.2 23.8 %collective-permute-start.4 = (bf16[8,128,256]{2,1,0:T(8,128)(2,1)S(1)}, bf16[8,128,256]{2,1,0:T(8,128)(2,1)S(1)}, u32[]{:S(2)}, u32[]{:S(2)}) collective-permute-start(bf16[8,128,256]{2,1,0:T(8,128)(2,1)S(1)} %pad_maximum_fusion.1), channel_id=1, source_target_pairs={{0,16},{8,24},{16,0},{24,8},{1,17},{9,25},{17,1},{25,9},{2,18},{10... | collective-permute-start | bytes 1572872 | tf_op jit(solution)/shard_map/ppermute | solution.py:45
  22.6 2.2 copy-start.10
  23.9 17.1 %collective-permute-start.3 = (bf16[8,128,256]{2,1,0:T(8,128)(2,1)S(1)}, bf16[8,128,256]{2,1,0:T(8,128)(2,1)S(1)}, u32[]{:S(2)}, u32[]{:S(2)}) collective-permute-start(bf16[8,128,256]{2,1,0:T(8,128)(2,1)S(1)} %pad_maximum_fusion.1), channel_id=1, source_target_pairs={{0,8},{8,16},{16,24},{24,0},{1,9},{9,17},{17,25},{25,1},{2,10},{10... | collective-permute-start | bytes 1572872 | tf_op jit(solution)/shard_map/ppermute | solution.py:45
  42.4 5.5 %copy-start.3 = (bf16[32,128,256]{2,1,0:T(8,128)(2,1)S(1)}, bf16[32,128,256]{2,1,0:T(8,128)(2,1)}, u32[]{:S(2)}) copy-start(bf16[32,128,256]{2,1,0:T(8,128)(2,1)} %pad_maximum_fusion) | copy-start | bytes 6291460
  44.6 0.6 copy-start.12
  47.7 6.5 %copy-start.2 = (bf16[256,4096]{1,0:T(8,128)(2,1)S(1)}, bf16[256,4096]{1,0:T(8,128)(2,1)}, u32[]{:S(2)}) copy-start(bf16[256,4096]{1,0:T(8,128)(2,1)} %all-gather.2.cloned.1.call-done) | copy-start | bytes 6291460
  47.8 6.5 %collective-permute-start.6 = (bf16[256,128]{0,1:T(8,128)(2,1)S(1)}, bf16[256,128]{0,1:T(8,128)(2,1)S(1)}, u32[]{:S(2)}, u32[]{:S(2)}) collective-permute-start(bf16[256,128]{0,1:T(8,128)(2,1)S(1)} %convolution_convert_fusion.2), channel_id=1, source_target_pairs={{0,1},{1,2},{2,3},{3,4},{4,5},{5,6},{6,7},{7,0},{8,9},{9,10},{10,1... | collective-permute-start | bytes 196616 | tf_op jit(solution)/shard_map/ppermute | solution.py:102
  50.7 9.5 %collective-permute-start.10 = (bf16[256,128]{0,1:T(8,128)(2,1)S(1)}, bf16[256,128]{0,1:T(8,128)(2,1)}, u32[]{:S(2)}, u32[]{:S(2)}) collective-permute-start(bf16[256,128]{0,1:T(8,128)(2,1)S(1)} %convolution_convert_fusion.2), channel_id=1, source_target_pairs={{0,7},{1,0},{2,1},{3,2},{4,3},{5,4},{6,5},{7,6},{8,15},{9,8},{10,9... | collective-permute-start | bytes 196616 | tf_op jit(solution)/shard_map/ppermute | solution.py:104
  54.2 5.6 %collective-permute-start.7 = (bf16[256,128]{0,1:T(8,128)(2,1)S(1)}, bf16[256,128]{0,1:T(8,128)(2,1)}, u32[]{:S(2)}, u32[]{:S(2)}) collective-permute-start(bf16[256,128]{0,1:T(8,128)(2,1)S(1)} %collective-permute-done.6), channel_id=1, source_target_pairs={{0,1},{1,2},{2,3},{3,4},{4,5},{5,6},{6,7},{7,0},{8,9},{9,10},{10,1... | collective-permute-start | bytes 196616 | tf_op jit(solution)/shard_map/ppermute | solution.py:102
  59.8 6.0 %collective-permute-start.8 = (bf16[256,128]{0,1:T(8,128)(2,1)}, bf16[256,128]{0,1:T(8,128)(2,1)S(1)}, u32[]{:S(2)}, u32[]{:S(2)}) collective-permute-start(bf16[256,128]{0,1:T(8,128)(2,1)} %collective-permute-done.7), channel_id=1, source_target_pairs={{0,1},{1,2},{2,3},{3,4},{4,5},{5,6},{6,7},{7,0},{8,9},{9,10},{10,1... | collective-permute-start | bytes 196616 | tf_op jit(solution)/shard_map/ppermute | solution.py:102
  60.2 6.6 %collective-permute-start.11 = (bf16[256,128]{0,1:T(8,128)(2,1)}, bf16[256,128]{0,1:T(8,128)(2,1)S(1)}, u32[]{:S(2)}, u32[]{:S(2)}) collective-permute-start(bf16[256,128]{0,1:T(8,128)(2,1)} %collective-permute-done.10), channel_id=1, source_target_pairs={{0,7},{1,0},{2,1},{3,2},{4,3},{5,4},{6,5},{7,6},{8,15},{9,8},{10,9... | collective-permute-start | bytes 196616 | tf_op jit(solution)/shard_map/ppermute | solution.py:104
  65.8 5.5 %collective-permute-start.9 = (bf16[256,128]{0,1:T(8,128)(2,1)S(1)}, bf16[256,128]{0,1:T(8,128)(2,1)S(1)}, u32[]{:S(2)}, u32[]{:S(2)}) collective-permute-start(bf16[256,128]{0,1:T(8,128)(2,1)S(1)} %collective-permute-done.8), channel_id=1, source_target_pairs={{0,1},{1,2},{2,3},{3,4},{4,5},{5,6},{6,7},{7,0},{8,9},{9,10},{10,1... | collective-permute-start | bytes 196616 | tf_op jit(solution)/shard_map/ppermute | solution.py:102
  66.8 6.4 %collective-permute-start.12 = (bf16[256,128]{0,1:T(8,128)(2,1)S(1)}, bf16[256,128]{0,1:T(8,128)(2,1)S(1)}, u32[]{:S(2)}, u32[]{:S(2)}) collective-permute-start(bf16[256,128]{0,1:T(8,128)(2,1)S(1)} %collective-permute-done.11), channel_id=1, source_target_pairs={{0,7},{1,0},{2,1},{3,2},{4,3},{5,4},{6,5},{7,6},{8,15},{9,8},{10,9... | collective-permute-start | bytes 196616 | tf_op jit(solution)/shard_map/ppermute | solution.py:104
  71.3 10.7 %copy-start.5 = (bf16[32,128,128]{2,1,0:T(8,128)(2,1)S(1)}, bf16[32,128,128]{2,1,0:T(8,128)(2,1)}, u32[]{:S(2)}) copy-start(bf16[32,128,128]{2,1,0:T(8,128)(2,1)} %get-tuple-element.7) | copy-start | bytes 3145732
  91.8 18.7 %copy-start.8 = (bf16[4096,128]{0,1:T(8,128)(2,1)S(1)}, bf16[4096,128]{0,1:T(8,128)(2,1)}, u32[]{:S(2)}) copy-start(bf16[4096,128]{0,1:T(8,128)(2,1)} %copy.25) | copy-start | bytes 3145732
  110.5 5.0 %copy-start.4 = (bf16[512,4096]{1,0:T(8,128)(2,1)S(1)}, bf16[512,4096]{1,0:T(8,128)(2,1)}, u32[]{:S(2)}) copy-start(bf16[512,4096]{1,0:T(8,128)(2,1)} %param.19) | copy-start | bytes 12582916
  115.5 2.7 %copy-start.9 = (bf16[4096]{0:T(1024)(128)(2,1)S(1)}, bf16[4096]{0:T(1024)(128)(2,1)}, u32[]{:S(2)}) copy-start(bf16[4096]{0:T(1024)(128)(2,1)} %param.16) | copy-start | bytes 24580
  118.2 132.1 %reduce-scatter.2.cloned.1.call-start = ((), (), s32[]{:S(2)}) async-start(), calls=%async_computation.3 | async-start | bytes 2359296 | tf_op jit(solution)/shard_map/reduce_scatter | solution.py:148
  185.2 1.3 copy-start.6
  192.9 22.0 %copy-start.7 = (bf16[256,512]{0,1:T(8,128)(2,1)S(1)}, bf16[256,512]{0,1:T(8,128)(2,1)}, u32[]{:S(2)}) copy-start(bf16[256,512]{0,1:T(8,128)(2,1)} %get-tuple-element.14) | copy-start | bytes 786436
  192.9 22.0 %copy-start.11 = (pred[256]{0:T(512)(128)(4,1)S(1)}, pred[256]{0:T(512)(128)(4,1)}, u32[]{:S(2)}) copy-start(pred[256]{0:T(512)(128)(4,1)} %copy-done.10) | copy-start | bytes 772
  192.9 59.2 %copy-start.1 = (bf16[4096,128]{1,0:T(8,128)(2,1)S(1)}, bf16[4096,128]{1,0:T(8,128)(2,1)}, u32[]{:S(2)}) copy-start(bf16[4096,128]{1,0:T(8,128)(2,1)} %param.18) | copy-start | bytes 3145732
Sparse Core Ops, SparseCore 0:
  9.6 31.7 all-gather.1
  118.3 64.2 all-reduce.1
  214.8 35.3 reduce-scatter.1
